TPU v7x, 512 devices: a whole 4x8x8 slice. The times are simulated.
512 devices in a mesh: feat: 16 (over x, z_hi, core), samp: 32 (over y, z_lo).
Axes of the slice: x: 4, y: 8, z: 8 (z_hi: 2, z_lo: 4; z = z_hi * 4 + z_lo), core: 2. Of those that a mesh axis runs over, the one named last changes fastest.
Arguments:
- tier_one: bfloat16 [8192, 12288], P('feat', 'samp')
- residuals: bfloat16 [12288, 128], P('samp'), may hold values from -6 to 6
- pair_list: int32 [3, 65536], P(None, 'feat'), may hold values from 0 to 8191, as said below
Outputs:
- scores: float32 [65536, 128], P(('feat', 'samp'))
Inputs may be any that keep to these rules, and one draw needn't show every extreme that they name: `pair_list`: rows 0 and 1 are feature indices, row 2 an operator id of 0 to 3; each descriptor's two features differ.
All inputs are finite; a program needn't handle non-finite values.
Results may differ from a plain program's by a relative error of at most 0.0031.
Values may be sent and summed in bfloat16 or wider, within the bound.
No kernel may reach another device: no remote copies, remote signals or barrier semaphores. Data moves between devices by JAX's collectives and lax.ppermute only.
A program may use at most 64 MiB of HBM per device.

v0:
```python
import math
import jax
import jax.numpy as jnp
from jax import lax
from jax.sharding import PartitionSpec as P

epsilon = 1e-05


def combine_rows(first_rows, second_rows, operator_id):
    first_rows = first_rows.astype(jnp.float32)
    second_rows = second_rows.astype(jnp.float32)
    quotient = first_rows / (1.0 + jnp.abs(second_rows))
    built = jnp.where(
        operator_id == 0,
        first_rows + second_rows,
        jnp.where(
            operator_id == 1,
            first_rows - second_rows,
            jnp.where(operator_id == 2, first_rows * second_rows, quotient),
        ),
    )
    return built.astype(jnp.bfloat16)


def descriptors(tier_one, pair_cols):
    first_rows = jnp.take(tier_one, pair_cols[0], axis=0)
    second_rows = jnp.take(tier_one, pair_cols[1], axis=0)
    return combine_rows(first_rows, second_rows, pair_cols[2][:, None])


def project_block(built, residuals):
    product = jnp.dot(built, residuals, preferred_element_type=jnp.float32)
    widened = built.astype(jnp.float32)
    return (product, jnp.sum(widened, axis=1), jnp.sum(widened * widened, axis=1))


def block_terms(tier_one, residuals, pair_cols):
    return project_block(descriptors(tier_one, pair_cols), residuals)


def finish(product, first_sums, square_sums, col_totals, sample_count):
    means = first_sums / sample_count
    variance = square_sums / sample_count - means * means
    centred = product - means[:, None] * col_totals[None, :]
    return centred * lax.rsqrt(variance + epsilon)[:, None] / math.sqrt(sample_count)


def per_device(tier_one, residuals, pair_list):
    local_pairs = pair_list.shape[1]
    width_k = residuals.shape[1]
    block_size = math.gcd(local_pairs, 1024)
    block_count = local_pairs // block_size
    grouped = pair_list.reshape(3, block_count, block_size).transpose(1, 0, 2)
    whole_rows = lax.all_gather(tier_one, "feat", axis=0, tiled=True)
    product, first_sums, square_sums = lax.map(
        lambda pair_cols: block_terms(whole_rows, residuals, pair_cols), grouped
    )
    product = product.reshape(local_pairs, width_k)
    first_sums = first_sums.reshape(local_pairs)
    square_sums = square_sums.reshape(local_pairs)
    col_totals = jnp.sum(residuals.astype(jnp.float32), axis=0)
    sample_count = residuals.shape[0] * lax.axis_size("samp")
    first_sums, square_sums, col_totals = lax.psum((first_sums, square_sums, col_totals), "samp")
    owned = lax.psum_scatter(product, "samp", scatter_dimension=0, tiled=True)
    owned_rows = owned.shape[0]
    row_start = lax.axis_index("samp") * owned_rows
    first_sums = lax.dynamic_slice_in_dim(first_sums, row_start, owned_rows, 0)
    square_sums = lax.dynamic_slice_in_dim(square_sums, row_start, owned_rows, 0)
    return finish(owned, first_sums, square_sums, col_totals, sample_count)


def solution(mesh):
    in_specs = (P("feat", "samp"), P("samp", None), P(None, "feat"))
    out_specs = P(("feat", "samp"), None)
    return jax.shard_map(
        per_device, mesh=mesh, in_specs=in_specs, out_specs=out_specs, check_vma=False
    )
```

profile of v0, /device:TPU:6, one launch (start us, length us, event | category | flops | bytes accessed | tf_op | source)
XLA Modules:
  0.0 361.1 jit_solution(16862348691693398649)
XLA Ops:
  7.3 105.8 %all-gather.2.cloned.1.call-done = bf16[8192,384]{1,0:T(8,128)(2,1)} async-done(((bf16[512,384]{1,0:T(8,128)(2,1)}), bf16[8192,384]{1,0:T(8,128)(2,1)}) %all-gather.2.cloned.1.call-update) | async-done | bytes 6291472 | tf_op jit(solution)/shard_map/all_gather | solution.py:55
  113.1 78.5 %while.14 = (s32[]{:T(128)}, f32[4,1024,128]{2,1,0:T(8,128)}, f32[4,1024]{1,0:T(4,128)S(1)}, f32[4,1024]{1,0:T(4,128)S(1)}, s32[4,3,1024]{2,1,0:T(4,128)}, /*ind...) while((s32[]{:T(128)}, f32[4,1024,128]{2,1,0:T(8,128)}, ...), condition=%wide.region_3.5_spmd, body=%wide.region_0.4_spmd.sunk | while | flops 107762688 | bytes 7395525 | solution.py:56
  113.9 0.8 constant_dynamic-slice_fusion.4
  114.7 7.4 %gather_fusion = bf16[1024,384]{1,0:T(8,128)(2,1)S(1)} fusion(bf16[8192,384]{1,0:T(8,128)(2,1)} %get-tuple-element.169, s32[1024]{0:T(1024)S(1)} %fusion.20), kind=kCustom, calls=%fused_computation.1.clone.clone.1 | custom fusion | bytes 1576960 | tf_op jit(solution)/shard_map/while/body/eval_jaxpr/jit(_take)/gather | solution.py:28
  122.1 7.4 %gather_fusion.1 = bf16[1024,384]{1,0:T(8,128)(2,1)S(1)} fusion(bf16[8192,384]{1,0:T(8,128)(2,1)} %get-tuple-element.169, s32[1024]{0:T(1024)S(1)} %fusion.21), kind=kCustom, calls=%fused_computation.clone.clone.1 | custom fusion | bytes 1576960 | tf_op jit(solution)/shard_map/while/body/eval_jaxpr/jit(_take)/gather | solution.py:27
  129.5 1.9 fusion.22
  131.5 1.2 fusion.23
  133.5 0.8 constant_dynamic-slice_fusion.4
  134.3 7.4 %gather_fusion = bf16[1024,384]{1,0:T(8,128)(2,1)S(1)} fusion(bf16[8192,384]{1,0:T(8,128)(2,1)} %get-tuple-element.169, s32[1024]{0:T(1024)S(1)} %fusion.20), kind=kCustom, calls=%fused_computation.1.clone.clone.1 | custom fusion | bytes 1576960 | tf_op jit(solution)/shard_map/while/body/eval_jaxpr/jit(_take)/gather | solution.py:28
  141.7 7.4 %gather_fusion.1 = bf16[1024,384]{1,0:T(8,128)(2,1)S(1)} fusion(bf16[8192,384]{1,0:T(8,128)(2,1)} %get-tuple-element.169, s32[1024]{0:T(1024)S(1)} %fusion.21), kind=kCustom, calls=%fused_computation.clone.clone.1 | custom fusion | bytes 1576960 | tf_op jit(solution)/shard_map/while/body/eval_jaxpr/jit(_take)/gather | solution.py:27
  149.1 1.9 fusion.22
  151.1 1.2 fusion.23
  154.0 7.4 %gather_fusion = bf16[1024,384]{1,0:T(8,128)(2,1)S(1)} fusion(bf16[8192,384]{1,0:T(8,128)(2,1)} %get-tuple-element.169, s32[1024]{0:T(1024)S(1)} %fusion.20), kind=kCustom, calls=%fused_computation.1.clone.clone.1 | custom fusion | bytes 1576960 | tf_op jit(solution)/shard_map/while/body/eval_jaxpr/jit(_take)/gather | solution.py:28
  161.3 7.4 %gather_fusion.1 = bf16[1024,384]{1,0:T(8,128)(2,1)S(1)} fusion(bf16[8192,384]{1,0:T(8,128)(2,1)} %get-tuple-element.169, s32[1024]{0:T(1024)S(1)} %fusion.21), kind=kCustom, calls=%fused_computation.clone.clone.1 | custom fusion | bytes 1576960 | tf_op jit(solution)/shard_map/while/body/eval_jaxpr/jit(_take)/gather | solution.py:27
  168.7 1.9 fusion.22
  170.8 1.2 fusion.23
  173.5 7.4 %gather_fusion = bf16[1024,384]{1,0:T(8,128)(2,1)S(1)} fusion(bf16[8192,384]{1,0:T(8,128)(2,1)} %get-tuple-element.169, s32[1024]{0:T(1024)S(1)} %fusion.20), kind=kCustom, calls=%fused_computation.1.clone.clone.1 | custom fusion | bytes 1576960 | tf_op jit(solution)/shard_map/while/body/eval_jaxpr/jit(_take)/gather | solution.py:28
  180.9 7.4 %gather_fusion.1 = bf16[1024,384]{1,0:T(8,128)(2,1)S(1)} fusion(bf16[8192,384]{1,0:T(8,128)(2,1)} %get-tuple-element.169, s32[1024]{0:T(1024)S(1)} %fusion.21), kind=kCustom, calls=%fused_computation.clone.clone.1 | custom fusion | bytes 1576960 | tf_op jit(solution)/shard_map/while/body/eval_jaxpr/jit(_take)/gather | solution.py:27
  188.3 1.9 fusion.22
  190.4 1.2 fusion.23
  191.6 0.9 copy-done.1
  192.5 151.1 %all-reduce = (f32[4096]{0:T(1024)S(1)}, f32[4096]{0:T(1024)S(1)}, f32[128]{0:T(128)S(1)}) all-reduce(f32[4096]{0:T(1024)S(1)} %get-tuple-element.77, f32[4096]{0:T(1024)S(1)} %get-tuple-element.78, f32[128]{0:T(128)S(1)} %convert_reduce_fusion.1), channel_id=1, replica_groups=mesh['feat'=16,'samp'=32] {'samp'}, use_global_device_ids=true, to_apply=%region_8.10 | all-reduce | flops 8320 | bytes 66560 | tf_op jit(solution)/shard_map/psum | solution.py:64
  343.7 9.1 %reduce-scatter.2.cloned.1.call-done = f32[128,128]{1,0:T(8,128)} async-done(((f32[4096,128]{1,0:T(8,128)}), f32[128,128]{1,0:T(8,128)}) %reduce-scatter.2.cloned.1.call-update) | async-done | bytes 65552 | tf_op jit(solution)/shard_map/reduce_scatter | solution.py:65
  352.7 1.6 multiply_multiply_fusion
  (45 shorter events, 6.3 us)
Async XLA Ops:
  6.5 106.6 %all-gather.2.cloned.1.call-start = ((), (), s32[]{:S(2)}) async-start(), calls=%async_computation.1 | async-start | bytes 6684672 | tf_op jit(solution)/shard_map/all_gather | solution.py:55
  7.3 345.5 %reduce-scatter.2.cloned.1.call-start = ((), (), s32[]{:S(2)}) async-start(), calls=%async_computation.2 | async-start | bytes 2162688 | tf_op jit(solution)/shard_map/reduce_scatter | solution.py:65
  129.5 2.1 copy-start
  149.1 2.1 copy-start
  168.7 2.1 copy-start
  188.3 2.1 copy-start
  191.6 0.9 copy-start.1
Sparse Core Ops, SparseCore 0:
  10.6 102.4 all-gather.1
  191.7 160.9 reduce-scatter.1
where the time goes:
time: 362 us; the launch traced here: 361 us
  blocking collectives  151 us (42%)
  waiting for transfers between devices  116 us (32%)
  local copies, waits for them, and re-layouts  63.7 us (18%)
  between operations  13.4 us (4%)
  other arithmetic  12.4 us (3%)
  matrix products  4.72 us (1%)
    psum x1, blocking collectives, per_device(): lax.psum((first_sums, square_sums, col_totals), 'samp')  151 us
    all_gather x1, waiting for transfers between devices, per_device(): whole_rows = lax.all_gather(tier_one, 'feat', axis=0, tiled=True)  106 us
    gather x4, local copies, waits for them, and re-layouts, descriptors(): second_rows = jnp.take(tier_one, pair_cols[1], axis=0)  29.5 us
    gather x4, local copies, waits for them, and re-layouts, descriptors(): first_rows = jnp.take(tier_one, pair_cols[0], axis=0)  29.5 us
    reduce_scatter x1, waiting for transfers between devices, per_device(): owned = lax.psum_scatter(product, 'samp', scatter_dimension=0, tiled=True)  9.07 us
    reduce_sum x4, other arithmetic, project_block(): jnp.sum(widened * widened, axis=1)  7.52 us
  transfers between devices with their start and end apart: 2, of which 2 were waited for; matrix products, arithmetic and copies ran while one was open for 0% of the time, Pallas kernels for 0%

commit v1 on v0

--- a/solution.py
+++ b/solution.py
@@ -52,7 +52,10 @@
     block_size = math.gcd(local_pairs, 1024)
     block_count = local_pairs // block_size
     grouped = pair_list.reshape(3, block_count, block_size).transpose(1, 0, 2)
-    whole_rows = lax.all_gather(tier_one, "feat", axis=0, tiled=True)
+    whole_rows = jnp.concatenate(
+        jax.lax.all_to_all(jnp.stack([tier_one] * jax.lax.axis_size("feat"), axis=0), "feat", 0, 0),
+        axis=0,
+    )
     product, first_sums, square_sums = lax.map(
         lambda pair_cols: block_terms(whole_rows, residuals, pair_cols), grouped
     )

time: 362 us -> 421 us (1.16)
  blocking collectives: 151 us -> 224 us
  waiting for transfers between devices: 116 us -> 84.7 us
  starting transfers between devices: 0.04 us -> 13.4 us
    all_gather x1 -> x0, waiting for transfers between devices: 106 us -> none  [per_device(): whole_rows = lax.all_gather(tier_one, 'feat', axis=0, tiled=True)]
    all_to_all x0 -> x1, waiting for transfers between devices: none -> 75.5 us  [per_device(): jax.lax.all_to_all(jnp.stack([tier_one] * jax.lax.axis_size('feat'), axis...]
    psum x1, blocking collectives: 151 us -> 224 us  [per_device(): lax.psum((first_sums, square_sums, col_totals), 'samp')]
    all_to_all x0 -> x1, starting transfers between devices: none -> 13.4 us  [per_device(): jax.lax.all_to_all(jnp.stack([tier_one] * jax.lax.axis_size('feat'), axis...]
    another operation x0 -> x1, local copies, waits for them, and re-layouts: none -> 4.46 us  [per_device(): jnp.stack([tier_one] * jax.lax.axis_size('feat'), axis=0)]
where the time goes in v1:
time: 421 us; the launch traced here: 420 us
  blocking collectives  224 us (53%)
  waiting for transfers between devices  84.7 us (20%)
  local copies, waits for them, and re-layouts  67.1 us (16%)
  starting transfers between devices  13.4 us (3%)
  between operations  13.4 us (3%)
  other arithmetic  12.4 us (3%)
  matrix products  4.75 us (1%)
    psum x1, blocking collectives, per_device(): lax.psum((first_sums, square_sums, col_totals), 'samp')  224 us
    all_to_all x1, waiting for transfers between devices, per_device(): jax.lax.all_to_all(jnp.stack([tier_one] * jax.lax.axis_size('feat'), axis...  75.5 us
    gather x4, local copies, waits for them, and re-layouts, descriptors(): second_rows = jnp.take(tier_one, pair_cols[1], axis=0)  29.5 us
    gather x4, local copies, waits for them, and re-layouts, descriptors(): first_rows = jnp.take(tier_one, pair_cols[0], axis=0)  29.5 us
    all_to_all x1, starting transfers between devices, per_device(): jax.lax.all_to_all(jnp.stack([tier_one] * jax.lax.axis_size('feat'), axis...  13.4 us
    reduce_scatter x1, waiting for transfers between devices, per_device(): owned = lax.psum_scatter(product, 'samp', scatter_dimension=0, tiled=True)  9.28 us
  transfers between devices with their start and end apart: 2, of which 2 were waited for; matrix products, arithmetic and copies ran while one was open for 0% of the time, Pallas kernels for 0%

profile of v1, /device:TPU:6, one launch (start us, length us, event | category | flops | bytes accessed | tf_op | source)
XLA Modules:
  0.0 419.8 jit_solution(9682175932418146393)
XLA Ops:
  6.5 4.5 %stack.2 = bf16[16,512,384]{2,1,0:T(8,128)(2,1)} broadcast(bf16[512,384]{1,0:T(8,128)(2,1)} %param.7), dimensions={1,2} | broadcast | bytes 6684672 | tf_op jit(solution)/shard_map/stack | solution.py:56
  11.0 13.4 %all-to-all-start = ((bf16[16,512,384]{2,1,0:T(8,128)(2,1)}), bf16[16,512,384]{2,1,0:T(8,128)(2,1)}, u32[]{:S(2)}, u32[]{:S(2)}) async-start(bf16[16,512,384]{2,1,0:T(8,128)(2,1)} %stack.2), calls=%async_computation | async-start | bytes 12582912 | tf_op jit(solution)/shard_map/all_to_all | solution.py:56
  24.4 75.5 %all-to-all-done = bf16[16,512,384]{2,1,0:T(8,128)(2,1)} async-done(((bf16[16,512,384]{2,1,0:T(8,128)(2,1)}), bf16[16,512,384]{2,1,0:T(8,128)(2,1)}, u32[]{:S(2)}, u32[]{:S(2)}) %all-to-all-start) | async-done | bytes 6291488 | tf_op jit(solution)/shard_map/all_to_all | solution.py:56
  99.9 78.4 %while.14 = (s32[]{:T(128)}, f32[4,1024,128]{2,1,0:T(8,128)}, f32[4,1024]{1,0:T(4,128)S(1)}, f32[4,1024]{1,0:T(4,128)S(1)}, s32[4,3,1024]{2,1,0:T(4,128)}, /*ind...) while((s32[]{:T(128)}, f32[4,1024,128]{2,1,0:T(8,128)}, ...), condition=%wide.region_3.5_spmd, body=%wide.region_0.4_spmd.sunk | while | flops 107762688 | bytes 7002781 | solution.py:59
  100.7 7.4 %gather_fusion = bf16[1024,384]{1,0:T(8,128)(2,1)S(1)} fusion(bf16[8192,384]{1,0:T(8,128)(2,1)} %get-tuple-element.169, s32[1024]{0:T(1024)S(1)} %fusion.20), kind=kCustom, calls=%fused_computation.1.clone.clone.1 | custom fusion | bytes 1576960 | tf_op jit(solution)/shard_map/while/body/eval_jaxpr/jit(_take)/gather | solution.py:28
  108.1 7.4 %gather_fusion.1 = bf16[1024,384]{1,0:T(8,128)(2,1)S(1)} fusion(bf16[8192,384]{1,0:T(8,128)(2,1)} %get-tuple-element.169, s32[1024]{0:T(1024)S(1)} %fusion.21), kind=kCustom, calls=%fused_computation.clone.clone.1 | custom fusion | bytes 1576960 | tf_op jit(solution)/shard_map/while/body/eval_jaxpr/jit(_take)/gather | solution.py:27
  116.3 1.9 fusion.22
  118.2 1.2 fusion.23
  120.3 7.4 %gather_fusion = bf16[1024,384]{1,0:T(8,128)(2,1)S(1)} fusion(bf16[8192,384]{1,0:T(8,128)(2,1)} %get-tuple-element.169, s32[1024]{0:T(1024)S(1)} %fusion.20), kind=kCustom, calls=%fused_computation.1.clone.clone.1 | custom fusion | bytes 1576960 | tf_op jit(solution)/shard_map/while/body/eval_jaxpr/jit(_take)/gather | solution.py:28
  127.7 7.4 %gather_fusion.1 = bf16[1024,384]{1,0:T(8,128)(2,1)S(1)} fusion(bf16[8192,384]{1,0:T(8,128)(2,1)} %get-tuple-element.169, s32[1024]{0:T(1024)S(1)} %fusion.21), kind=kCustom, calls=%fused_computation.clone.clone.1 | custom fusion | bytes 1576960 | tf_op jit(solution)/shard_map/while/body/eval_jaxpr/jit(_take)/gather | solution.py:27
  135.9 1.9 fusion.22
  137.8 1.2 fusion.23
  139.1 0.8 constant_dynamic-slice_fusion.4
  140.0 7.4 %gather_fusion = bf16[1024,384]{1,0:T(8,128)(2,1)S(1)} fusion(bf16[8192,384]{1,0:T(8,128)(2,1)} %get-tuple-element.169, s32[1024]{0:T(1024)S(1)} %fusion.20), kind=kCustom, calls=%fused_computation.1.clone.clone.1 | custom fusion | bytes 1576960 | tf_op jit(solution)/shard_map/while/body/eval_jaxpr/jit(_take)/gather | solution.py:28
  147.4 7.4 %gather_fusion.1 = bf16[1024,384]{1,0:T(8,128)(2,1)S(1)} fusion(bf16[8192,384]{1,0:T(8,128)(2,1)} %get-tuple-element.169, s32[1024]{0:T(1024)S(1)} %fusion.21), kind=kCustom, calls=%fused_computation.clone.clone.1 | custom fusion | bytes 1576960 | tf_op jit(solution)/shard_map/while/body/eval_jaxpr/jit(_take)/gather | solution.py:27
  155.5 1.9 fusion.22
  157.4 1.2 fusion.23
  159.6 7.4 %gather_fusion = bf16[1024,384]{1,0:T(8,128)(2,1)S(1)} fusion(bf16[8192,384]{1,0:T(8,128)(2,1)} %get-tuple-element.169, s32[1024]{0:T(1024)S(1)} %fusion.20), kind=kCustom, calls=%fused_computation.1.clone.clone.1 | custom fusion | bytes 1576960 | tf_op jit(solution)/shard_map/while/body/eval_jaxpr/jit(_take)/gather | solution.py:28
  166.9 7.4 %gather_fusion.1 = bf16[1024,384]{1,0:T(8,128)(2,1)S(1)} fusion(bf16[8192,384]{1,0:T(8,128)(2,1)} %get-tuple-element.169, s32[1024]{0:T(1024)S(1)} %fusion.21), kind=kCustom, calls=%fused_computation.clone.clone.1 | custom fusion | bytes 1576960 | tf_op jit(solution)/shard_map/while/body/eval_jaxpr/jit(_take)/gather | solution.py:27
  175.1 1.9 fusion.22
  177.0 1.2 fusion.23
  178.4 223.6 %all-reduce = (f32[4096]{0:T(1024)S(1)}, f32[4096]{0:T(1024)S(1)}, f32[128]{0:T(128)S(1)}) all-reduce(f32[4096]{0:T(1024)S(1)} %get-tuple-element.77, f32[4096]{0:T(1024)S(1)} %get-tuple-element.78, f32[128]{0:T(128)S(1)} %convert_reduce_fusion.1), channel_id=1, replica_groups=mesh['feat'=16,'samp'=32] {'samp'}, use_global_device_ids=true, to_apply=%region_8.10 | all-reduce | flops 8320 | bytes 66560 | tf_op jit(solution)/shard_map/psum | solution.py:67
  402.1 9.3 %reduce-scatter.2.cloned.1.call-done = f32[128,128]{1,0:T(8,128)} async-done(((f32[4096,128]{1,0:T(8,128)}), f32[128,128]{1,0:T(8,128)}) %reduce-scatter.2.cloned.1.call-update) | async-done | bytes 65552 | tf_op jit(solution)/shard_map/reduce_scatter | solution.py:68
  411.3 1.6 multiply_multiply_fusion
  (37 shorter events, 6.3 us)
Async XLA Ops:
  11.0 88.9 %copy-start = (bf16[384,128]{1,0:T(8,128)(2,1)S(1)}, bf16[384,128]{1,0:T(8,128)(2,1)}, u32[]{:S(2)}) copy-start(bf16[384,128]{1,0:T(8,128)(2,1)} %param.8) | copy-start | bytes 294916
  11.0 88.9 %all-to-all-start = ((bf16[16,512,384]{2,1,0:T(8,128)(2,1)}), bf16[16,512,384]{2,1,0:T(8,128)(2,1)}, u32[]{:S(2)}, u32[]{:S(2)}) async-start(bf16[16,512,384]{2,1,0:T(8,128)(2,1)} %stack.2), calls=%async_computation | async-start | bytes 12582912 | tf_op jit(solution)/shard_map/all_to_all | solution.py:56
  24.4 387.0 %reduce-scatter.2.cloned.1.call-start = ((), (), s32[]{:S(2)}) async-start(), calls=%async_computation.2 | async-start | bytes 2162688 | tf_op jit(solution)/shard_map/reduce_scatter | solution.py:68
Sparse Core Ops, SparseCore 0:
  178.4 232.8 reduce-scatter.1
